TPU v7x, 512 devices: a whole 4x8x8 slice. The times are simulated.
512 devices in a mesh: segment: 8 (over z), gy: 64 (over x, y, core).
Axes of the slice: x: 4, y: 8, z: 8, core: 2. Of those that a mesh axis runs over, the one named last changes fastest.
Arguments:
- acts: bfloat16 [8, 8, 128, 32, 256], P('segment', None, 'gy'), may hold values from -6 to 6
- grad_out: bfloat16 [8, 128, 32, 256], P('segment', 'gy'), may hold values from -6 to 6
- w_plane: bfloat16 [8, 3, 3, 32, 32], P('segment'), may hold values from -0.375 to 0.375
- w_depth: bfloat16 [8, 3, 32, 32], P('segment'), may hold values from -0.625 to 0.625
- tiles: int32 [64, 12], P('gy'), may hold values from -1 to 15, as said below
Outputs:
- grad_in: bfloat16 [8, 128, 32, 256], P('segment', 'gy')
- grad_plane: float32 [8, 3, 3, 32, 32], P('segment')
- grad_depth: float32 [8, 3, 32, 32], P('segment')
Inputs may be any that keep to these rules, and one draw needn't show every extreme that they name: Row s lists distinct tiles z * 2 + x-tile of slab s in its first entries and -1 after them; each row lists 1 to 12 tiles, and some row lists exactly 12.
All inputs are finite; a program needn't handle non-finite values.
Results may differ from a plain program's by a relative error of at most 0.02.
Values may be sent and summed in bfloat16 or wider, within the bound.
No kernel may reach another device: no remote copies, remote signals or barrier semaphores. Data moves between devices by JAX's collectives and lax.ppermute only.
A program may use at most 64 MiB of HBM per device.

v0:
```python
import math
import jax
import jax.numpy as jnp
from jax import lax
from jax.sharding import PartitionSpec as P

TILE = 128


def padded_2(block, sides, width):
    for axis, dim in sides:
        count = lax.axis_size(axis)
        forward = [(i, i + 1) for i in range(count - 1)]
        backward = [(target, source) for source, target in forward]
        low = lax.ppermute(
            lax.slice_in_dim(block, block.shape[dim] - width, None, axis=dim), axis, forward
        )
        high = lax.ppermute(lax.slice_in_dim(block, 0, width, axis=dim), axis, backward)
        block = jnp.concatenate([low, block, high], axis=dim)
    return block


def width_pad(field):
    return jnp.pad(field, [(0, 0)] * (field.ndim - 1) + [(1, 1)])


def plane_conv_all(rows_in, kernel, height, width):
    padded = width_pad(rows_in)
    total = None
    for i in range(3):
        for j in range(3):
            term = jnp.einsum(
                "loc,lzycx->lzyox",
                kernel[:, i, j],
                padded[:, :, i : i + height, :, j : j + width],
                preferred_element_type=jnp.float32,
            )
            total = term if total is None else total + term
    return total


def depth_conv_all(deep, kernel, depth):
    total = None
    for k in range(3):
        term = jnp.einsum(
            "loc,lzycx->lzyox",
            kernel[:, k],
            deep[:, k : k + depth],
            preferred_element_type=jnp.float32,
        )
        total = term if total is None else total + term
    return total


def plane_back(rows_grad, kernel, height, width):
    padded = width_pad(rows_grad)
    total = None
    for i in range(3):
        for j in range(3):
            term = jnp.einsum(
                "oc,...yox->...ycx",
                kernel[i, j],
                padded[..., 2 - i : 2 - i + height, :, 2 - j : 2 - j + width],
                preferred_element_type=jnp.float32,
            )
            total = term if total is None else total + term
    return total


def plane_taps(grad_mid, rows_in, height, width):
    padded = width_pad(rows_in)
    rows_out = []
    for i in range(3):
        row_taps = []
        for j in range(3):
            row_taps.append(
                jnp.einsum(
                    "...yox,...ycx->oc",
                    grad_mid,
                    padded[..., i : i + height, :, j : j + width],
                    preferred_element_type=jnp.float32,
                )
            )
        rows_out.append(jnp.stack(row_taps))
    return jnp.stack(rows_out)


def depth_back(mix_deep, kernel, depth):
    total = None
    for k in range(3):
        term = jnp.einsum(
            "oc,zyox->zycx",
            kernel[k],
            mix_deep[2 - k : 2 - k + depth],
            preferred_element_type=jnp.float32,
        )
        total = term if total is None else total + term
    return total


def depth_taps(grad_mix, deep, depth):
    return jnp.stack(
        [
            jnp.einsum(
                "zyox,zycx->oc", grad_mix, deep[k : k + depth], preferred_element_type=jnp.float32
            )
            for k in range(3)
        ]
    )


def silu_slope(value):
    sig = jax.nn.sigmoid(value)
    return sig * (1.0 + value * (1.0 - sig))


def local(acts, grad_out, w_plane, w_depth, tiles):
    sections = acts.shape[1]
    height = acts.shape[2]
    width = acts.shape[4]
    chans = w_plane.shape[3]
    count = lax.axis_size("segment")
    layers = count * acts.shape[0]
    zs = grad_out.shape[0]
    scale = 1.0 / math.sqrt(sections * height * lax.axis_size("gy") * width)
    segment = lax.axis_index("segment")
    mine = lax.all_to_all(acts, "segment", 1, 0, tiled=True)
    plane_w = lax.all_gather(w_plane, "segment", axis=0, tiled=True)
    depth_w = lax.all_gather(w_depth, "segment", axis=0, tiled=True)
    ids = (segment * zs + jnp.arange(zs, dtype=jnp.int32))[:, None] * (width // TILE) + jnp.arange(
        width // TILE, dtype=jnp.int32
    )[None, :]
    hit = jnp.any(tiles[0][None, None, :] == ids[:, :, None], axis=2)
    mask_full = jnp.repeat(hit.astype(jnp.float32), TILE, axis=1)[:, None, None, :]
    rows_own = padded_2(mine, (("gy", 2),), 1)
    mid = plane_conv_all(rows_own, plane_w, height, width).astype(jnp.bfloat16)
    deep = padded_2(mid, (("segment", 1),), 1)
    value = depth_conv_all(deep, depth_w, zs)
    factor = silu_slope(value) * mask_full[None]
    grad = grad_out
    plane_list = [None] * layers
    depth_list = [None] * layers
    for layer in reversed(range(layers)):
        grad_mix = (grad.astype(jnp.float32) * factor[layer]).astype(jnp.bfloat16)
        mix_deep = padded_2(grad_mix, (("segment", 0),), 1)
        grad_mid = depth_back(mix_deep, depth_w[layer], zs).astype(jnp.bfloat16)
        rows_grad = padded_2(grad_mid, (("gy", 1),), 1)
        grad = (
            grad.astype(jnp.float32) + plane_back(rows_grad, plane_w[layer], height, width)
        ).astype(jnp.bfloat16)
        depth_list[layer] = depth_taps(grad_mix, deep[layer], zs)
        plane_list[layer] = plane_taps(grad_mid, rows_own[layer], height, width)
    planes = jnp.stack(plane_list).reshape(layers, -1)
    depths = jnp.stack(depth_list).reshape(layers, -1)
    flat = jnp.concatenate([planes, depths], axis=1) * scale
    flat = lax.psum_scatter(flat, "segment", scatter_dimension=0, tiled=True)
    flat = lax.psum(flat, "gy")
    cut = planes.shape[1]
    plane_sum = flat[:, :cut].reshape(-1, 3, 3, chans, chans)
    depth_sum = flat[:, cut:].reshape(-1, 3, chans, chans)
    return (grad, plane_sum, depth_sum)


def solution(mesh):
    placed = (
        P("segment", None, "gy", None, None),
        P("segment", "gy", None, None),
        P("segment", None, None, None, None),
        P("segment", None, None, None),
        P("gy", None),
    )
    return jax.shard_map(
        local,
        mesh=mesh,
        in_specs=placed,
        out_specs=(
            P("segment", "gy", None, None),
            P("segment", None, None, None, None),
            P("segment", None, None, None),
        ),
        check_vma=False,
    )
```

profile of v0, /device:TPU:64, one launch (start us, length us, event | category | flops | bytes accessed | tf_op | source)
XLA Modules:
  0.0 603.1 jit_solution(2332710889217415071)
XLA Ops:
  7.2 10.0 %all-to-all-start = ((bf16[1,8,2,32,256]{4,3,2,0,1:T(8,128)(2,1)}), bf16[1,8,2,32,256]{4,3,2,0,1:T(8,128)(2,1)S(1)}, u32[]{:S(2)}, u32[]{:S(2)}) async-start(bf16[1,8,2,32,256]{4,3,2,0,1:T(8,128)(2,1)} %bitcast.2011), calls=%async_computation | async-start | bytes 524288 | tf_op jit(solution)/shard_map/all_to_all | solution.py:127
  18.7 26.2 %all_gather.7 = bf16[8,3,32,32]{3,2,0,1:T(8,128)(2,1)S(1)} all-gather(bf16[1,3,32,32]{3,2,0,1:T(8,128)(2,1)S(1)} %bitcast.2013), channel_id=1, replica_groups=mesh['segment'=8,'gy'=64] {'segment'}, dimensions={0}, use_global_device_ids=true | all-gather | bytes 55296 | tf_op jit(solution)/shard_map/all_gather | solution.py:129
  44.9 25.8 %all_gather.6 = bf16[8,3,3,32,32]{4,3,0,2,1:T(8,128)(2,1)S(1)} all-gather(bf16[1,3,3,32,32]{4,3,0,2,1:T(8,128)(2,1)S(1)} %bitcast.2012), channel_id=1, replica_groups=mesh['segment'=8,'gy'=64] {'segment'}, dimensions={0}, use_global_device_ids=true | all-gather | bytes 165888 | tf_op jit(solution)/shard_map/all_gather | solution.py:128
  73.4 3.7 collective-permute-done.1
  81.4 3.9 collective-permute-start.2
  90.4 4.2 collective-permute-start.5
  97.3 3.2 collective-permute-done.4
  102.3 3.2 collective-permute-start.6
  107.0 5.1 collective-permute-done.7
  114.2 5.6 collective-permute-start.9
  122.3 4.4 collective-permute-done.8
  128.6 3.2 collective-permute-start.10
  137.7 3.9 collective-permute-start.13
  144.2 3.2 collective-permute-done.12
  149.2 3.0 collective-permute-start.14
  158.3 3.1 collective-permute-start.17
  161.5 2.7 collective-permute-start.16
  169.1 3.0 collective-permute-start.18
  178.2 3.1 collective-permute-start.21
  181.3 2.7 collective-permute-start.20
  189.0 3.0 collective-permute-start.22
  198.3 3.1 collective-permute-start.25
  201.4 2.7 collective-permute-start.24
  209.0 3.0 collective-permute-start.26
  213.5 3.8 collective-permute-done.27
  219.3 3.1 collective-permute-start.29
  230.1 3.0 collective-permute-start.30
  234.6 3.8 collective-permute-done.31
  240.4 3.1 collective-permute-start.33
  251.4 3.0 collective-permute-start.34
  262.1 84.7 %all-reduce.20.cloned.1.call-done = f32[8,12288]{1,0:T(8,128)} async-done(((f32[8,12288]{1,0:T(8,128)}), f32[8,12288]{1,0:T(8,128)}) %all-reduce.20.cloned.1.call-update) | async-done | bytes 393232
  348.5 246.2 %psum.7 = f32[1,12288]{1,0:T(1,128)S(1)} all-reduce(f32[1,12288]{1,0:T(1,128)S(1)} %constant_dynamic-slice_fusion), channel_id=1, replica_groups=mesh['segment'=8,'gy'=64] {'gy'}, use_global_device_ids=true, to_apply=%region_2.3 | all-reduce | flops 12288 | bytes 98304 | tf_op jit(solution)/shard_map/psum | solution.py:157
  (342 shorter events, 102.5 us)
Async XLA Ops:
  7.2 63.5 %all-to-all-start = ((bf16[1,8,2,32,256]{4,3,2,0,1:T(8,128)(2,1)}), bf16[1,8,2,32,256]{4,3,2,0,1:T(8,128)(2,1)S(1)}, u32[]{:S(2)}, u32[]{:S(2)}) async-start(bf16[1,8,2,32,256]{4,3,2,0,1:T(8,128)(2,1)} %bitcast.2011), calls=%async_computation | async-start | bytes 524288 | tf_op jit(solution)/shard_map/all_to_all | solution.py:127
  17.2 329.7 %all-reduce.20.cloned.1.call-start = ((), (), s32[]{:S(2)}) async-start(), calls=%async_computation.1 | async-start | bytes 786432
  72.0 5.0 collective-permute-start.1
  79.5 8.4 %collective-permute-start.3 = (bf16[8,1,2,32,256]{4,3,2,0,1:T(8,128)(2,1)S(1)}, bf16[8,1,2,32,256]{4,3,2,0,1:T(8,128)(2,1)S(1)}, u32[]{:S(2)}, u32[]{:S(2)}) collective-permute-start(bf16[8,1,2,32,256]{4,3,2,0,1:T(8,128)(2,1)S(1)} %bitcast.1994), channel_id=1, source_target_pairs={{64,0},{128,64},{192,128},{256,192},{320,256},{384,320},{448,384},... | collective-permute-start | bytes 786440 | tf_op jit(solution)/shard_map/ppermute | solution.py:18
  81.4 8.4 %collective-permute-start.2 = (bf16[8,1,2,32,256]{4,3,2,0,1:T(8,128)(2,1)S(1)}, bf16[8,1,2,32,256]{4,3,2,0,1:T(8,128)(2,1)S(1)}, u32[]{:S(2)}, u32[]{:S(2)}) collective-permute-start(bf16[8,1,2,32,256]{4,3,2,0,1:T(8,128)(2,1)S(1)} %bitcast.1995), channel_id=1, source_target_pairs={{0,64},{64,128},{128,192},{192,256},{256,320},{320,384},{384,448},... | collective-permute-start | bytes 786440 | tf_op jit(solution)/shard_map/ppermute | solution.py:15
  90.4 6.6 %collective-permute-start.5 = (bf16[1,2,32,256]{3,2,1,0:T(8,128)(2,1)S(1)}, bf16[1,2,32,256]{3,2,1,0:T(8,128)(2,1)S(1)}, u32[]{:S(2)}, u32[]{:S(2)}) collective-permute-start(bf16[1,2,32,256]{3,2,1,0:T(8,128)(2,1)S(1)} %fusion.86), channel_id=1, source_target_pairs={{0,64},{64,128},{128,192},{192,256},{256,320},{320,384},{384,448},... | collective-permute-start | bytes 98312 | tf_op jit(solution)/shard_map/ppermute | solution.py:15
  94.6 5.8 collective-permute-start.4
  102.3 4.7 collective-permute-start.6
  105.5 6.6 %collective-permute-start.7 = (bf16[1,1,32,256]{3,2,1,0:T(8,128)(2,1)S(1)}, bf16[1,1,32,256]{3,2,1,0:T(8,128)(2,1)S(1)}, u32[]{:S(2)}, u32[]{:S(2)}) collective-permute-start(bf16[1,1,32,256]{3,2,1,0:T(8,128)(2,1)S(1)} %get-tuple-element.36), channel_id=1, source_target_pairs={{1,0},{2,1},{3,2},{4,3},{5,4},{6,5},{7,6},{8,7},{9,8},{10,9},{11,1... | collective-permute-start | bytes 49160 | tf_op jit(solution)/shard_map/ppermute | solution.py:18
  114.2 8.0 %collective-permute-start.9 = (bf16[1,2,32,256]{3,2,1,0:T(8,128)(2,1)S(1)}, bf16[1,2,32,256]{3,2,1,0:T(8,128)(2,1)S(1)}, u32[]{:S(2)}, u32[]{:S(2)}) collective-permute-start(bf16[1,2,32,256]{3,2,1,0:T(8,128)(2,1)S(1)} %get-tuple-element.37), channel_id=1, source_target_pairs={{0,64},{64,128},{128,192},{192,256},{256,320},{320,384},{384,448},... | collective-permute-start | bytes 98312 | tf_op jit(solution)/shard_map/ppermute | solution.py:15
  119.7 7.0 %collective-permute-start.8 = (bf16[1,2,32,256]{3,2,1,0:T(8,128)(2,1)S(1)}, bf16[1,2,32,256]{3,2,1,0:T(8,128)(2,1)S(1)}, u32[]{:S(2)}, u32[]{:S(2)}) collective-permute-start(bf16[1,2,32,256]{3,2,1,0:T(8,128)(2,1)S(1)} %get-tuple-element.37), channel_id=1, source_target_pairs={{64,0},{128,64},{192,128},{256,192},{320,256},{384,320},{448,384},... | collective-permute-start | bytes 98312 | tf_op jit(solution)/shard_map/ppermute | solution.py:18
  128.6 4.7 collective-permute-start.10
  137.7 6.4 %collective-permute-start.13 = (bf16[1,2,32,256]{3,2,1,0:T(8,128)(2,1)S(1)}, bf16[1,2,32,256]{3,2,1,0:T(8,128)(2,1)S(1)}, u32[]{:S(2)}, u32[]{:S(2)}) collective-permute-start(bf16[1,2,32,256]{3,2,1,0:T(8,128)(2,1)S(1)} %get-tuple-element.39), channel_id=1, source_target_pairs={{0,64},{64,128},{128,192},{192,256},{256,320},{320,384},{384,448},... | collective-permute-start | bytes 98312 | tf_op jit(solution)/shard_map/ppermute | solution.py:15
  141.6 5.8 collective-permute-start.12
  149.2 4.4 collective-permute-start.14
  158.3 6.3 %collective-permute-start.17 = (bf16[1,2,32,256]{3,2,1,0:T(8,128)(2,1)S(1)}, bf16[1,2,32,256]{3,2,1,0:T(8,128)(2,1)S(1)}, u32[]{:S(2)}, u32[]{:S(2)}) collective-permute-start(bf16[1,2,32,256]{3,2,1,0:T(8,128)(2,1)S(1)} %get-tuple-element.41), channel_id=1, source_target_pairs={{0,64},{64,128},{128,192},{192,256},{256,320},{320,384},{384,448},... | collective-permute-start | bytes 98312 | tf_op jit(solution)/shard_map/ppermute | solution.py:15
  161.5 5.8 collective-permute-start.16
  169.1 4.4 collective-permute-start.18
  178.2 6.3 %collective-permute-start.21 = (bf16[1,2,32,256]{3,2,1,0:T(8,128)(2,1)S(1)}, bf16[1,2,32,256]{3,2,1,0:T(8,128)(2,1)S(1)}, u32[]{:S(2)}, u32[]{:S(2)}) collective-permute-start(bf16[1,2,32,256]{3,2,1,0:T(8,128)(2,1)S(1)} %get-tuple-element.43), channel_id=1, source_target_pairs={{0,64},{64,128},{128,192},{192,256},{256,320},{320,384},{384,448},... | collective-permute-start | bytes 98312 | tf_op jit(solution)/shard_map/ppermute | solution.py:15
  181.3 5.8 collective-permute-start.20
  189.0 4.4 collective-permute-start.22
  198.3 6.3 %collective-permute-start.25 = (bf16[1,2,32,256]{3,2,1,0:T(8,128)(2,1)S(1)}, bf16[1,2,32,256]{3,2,1,0:T(8,128)(2,1)S(1)}, u32[]{:S(2)}, u32[]{:S(2)}) collective-permute-start(bf16[1,2,32,256]{3,2,1,0:T(8,128)(2,1)S(1)} %get-tuple-element.45), channel_id=1, source_target_pairs={{0,64},{64,128},{128,192},{192,256},{256,320},{320,384},{384,448},... | collective-permute-start | bytes 98312 | tf_op jit(solution)/shard_map/ppermute | solution.py:15
  201.4 5.8 collective-permute-start.24
  209.0 4.4 collective-permute-start.26
  212.0 5.2 collective-permute-start.27
  219.3 6.3 %collective-permute-start.29 = (bf16[1,2,32,256]{3,2,1,0:T(8,128)(2,1)S(1)}, bf16[1,2,32,256]{3,2,1,0:T(8,128)(2,1)S(1)}, u32[]{:S(2)}, u32[]{:S(2)}) collective-permute-start(bf16[1,2,32,256]{3,2,1,0:T(8,128)(2,1)S(1)} %get-tuple-element.47), channel_id=1, source_target_pairs={{0,64},{64,128},{128,192},{192,256},{256,320},{320,384},{384,448},... | collective-permute-start | bytes 98312 | tf_op jit(solution)/shard_map/ppermute | solution.py:15
  222.5 5.8 collective-permute-start.28
  233.1 5.2 collective-permute-start.31
  240.4 6.5 %collective-permute-start.33 = (bf16[1,2,32,256]{3,2,1,0:T(8,128)(2,1)S(1)}, bf16[1,2,32,256]{3,2,1,0:T(8,128)(2,1)S(1)}, u32[]{:S(2)}, u32[]{:S(2)}) collective-permute-start(bf16[1,2,32,256]{3,2,1,0:T(8,128)(2,1)S(1)} %get-tuple-element.49), channel_id=1, source_target_pairs={{0,64},{64,128},{128,192},{192,256},{256,320},{320,384},{384,448},... | collective-permute-start | bytes 98312 | tf_op jit(solution)/shard_map/ppermute | solution.py:15
  243.6 5.8 collective-permute-start.32
  251.4 5.6 collective-permute-start.34
  254.4 5.2 collective-permute-start.35
  (10 other events, 63.0 us)
Sparse Core Ops, SparseCore 0:
  257.1 89.6 all-reduce.19
where the time goes:
time: 604 us; the launch traced here: 603 us
  blocking collectives  298 us (49%)
  waiting for transfers between devices  140 us (23%)
  starting transfers between devices  101 us (17%)
  matrix products  38.6 us (6%)
  between operations  15.3 us (3%)
  local copies, waits for them, and re-layouts  7.11 us (1%)
    psum x1, blocking collectives, local(): flat = lax.psum(flat, 'gy')  246 us
    unnamed x2, waiting for transfers between devices  84.7 us
    ppermute x18, starting transfers between devices, padded_2(): lax.ppermute(lax.slice_in_dim(block, block.shape[dim] - width, None, axis...  58.6 us
    ppermute x18, waiting for transfers between devices, padded_2(): lax.ppermute(lax.slice_in_dim(block, 0, width, axis=dim), axis, backward)  53.8 us
    ppermute x18, starting transfers between devices, padded_2(): lax.ppermute(lax.slice_in_dim(block, 0, width, axis=dim), axis, backward)  32.9 us
    all_gather x1, blocking collectives, local(): depth_w = lax.all_gather(w_depth, 'segment', axis=0, tiled=True)  26.2 us
    all_gather x1, blocking collectives, local(): plane_w = lax.all_gather(w_plane, 'segment', axis=0, tiled=True)  25.8 us
    dot_general x72, matrix products, plane_back(): jnp.einsum('oc,...yox->...ycx', kernel[i, j], padded[..., 2 - i:2 - i + h...  15 us
  transfers between devices with their start and end apart: 38, of which 20 were waited for; matrix products, arithmetic and copies ran while one was open for 2% of the time, Pallas kernels for 0%

commit v1 on v0

--- a/solution.py
+++ b/solution.py
@@ -5,6 +5,19 @@
 from jax.sharding import PartitionSpec as P
 
 TILE = 128
+
+
+def ring_gather(x, axis, dim):
+    ways = lax.axis_size(axis)
+    up = [(d, (d + 1) % ways) for d in range(ways)]
+    down = [(d, (d - 1) % ways) for d in range(ways)]
+    earlier, later = ([x], [x])
+    for _ in range(ways // 2):
+        earlier.append(lax.ppermute(earlier[-1], axis, up))
+    for _ in range((ways - 1) // 2):
+        later.append(lax.ppermute(later[-1], axis, down))
+    line = jnp.concatenate([*earlier[::-1], *later[1:]], axis=dim)
+    return jnp.roll(line, (lax.axis_index(axis) - ways // 2) * x.shape[dim], axis=dim)
 
 
 def padded_2(block, sides, width):
@@ -125,7 +138,7 @@
     scale = 1.0 / math.sqrt(sections * height * lax.axis_size("gy") * width)
     segment = lax.axis_index("segment")
     mine = lax.all_to_all(acts, "segment", 1, 0, tiled=True)
-    plane_w = lax.all_gather(w_plane, "segment", axis=0, tiled=True)
+    plane_w = ring_gather(w_plane, "segment", 0)
     depth_w = lax.all_gather(w_depth, "segment", axis=0, tiled=True)
     ids = (segment * zs + jnp.arange(zs, dtype=jnp.int32))[:, None] * (width // TILE) + jnp.arange(
         width // TILE, dtype=jnp.int32

time: 604 us -> 611 us (1.012)
  blocking collectives: 298 us -> 274 us
  starting transfers between devices: 101 us -> 123 us
  waiting for transfers between devices: 140 us -> 148 us
    all_gather x1 -> x0, blocking collectives: 25.8 us -> none  [local(): plane_w = lax.all_gather(w_plane, 'segment', axis=0, tiled=True)]
    ppermute x0 -> x7, starting transfers between devices: none -> 23.3 us  [the longest x4 13.6 us: ring_gather(): earlier.append(lax.ppermute(earlier[-1], axis, up))]
    ppermute x0 -> x7, waiting for transfers between devices: none -> 7.03 us  [the longest x3 4.17 us: ring_gather(): later.append(lax.ppermute(later[-1], axis, down))]
  transfers between devices with their start and end apart: 38 -> 45, of which waited for: 20 -> 22; matrix products, arithmetic and copies ran while one was open for 2% -> 2% of each run, Pallas kernels for 0% -> 0%
where the time goes in v1:
time: 611 us; the launch traced here: 609 us
  blocking collectives  274 us (45%)
  waiting for transfers between devices  148 us (24%)
  starting transfers between devices  123 us (20%)
  matrix products  38.6 us (6%)
  between operations  15.4 us (3%)
  local copies, waits for them, and re-layouts  7.36 us (1%)
    psum x1, blocking collectives, local(): flat = lax.psum(flat, 'gy')  246 us
    unnamed x2, waiting for transfers between devices  84.7 us
    ppermute x18, starting transfers between devices, padded_2(): lax.ppermute(lax.slice_in_dim(block, block.shape[dim] - width, None, axis...  57.6 us
    ppermute x18, waiting for transfers between devices, padded_2(): lax.ppermute(lax.slice_in_dim(block, 0, width, axis=dim), axis, backward)  54.1 us
    ppermute x18, starting transfers between devices, padded_2(): lax.ppermute(lax.slice_in_dim(block, 0, width, axis=dim), axis, backward)  33.9 us
    all_gather x1, blocking collectives, local(): depth_w = lax.all_gather(w_depth, 'segment', axis=0, tiled=True)  27.8 us
    dot_general x72, matrix products, plane_back(): jnp.einsum('oc,...yox->...ycx', kernel[i, j], padded[..., 2 - i:2 - i + h...  14.9 us
    ppermute x4, starting transfers between devices, ring_gather(): earlier.append(lax.ppermute(earlier[-1], axis, up))  13.6 us
  transfers between devices with their start and end apart: 45, of which 22 were waited for; matrix products, arithmetic and copies ran while one was open for 2% of the time, Pallas kernels for 0%

profile of v1, /device:TPU:64, one launch (start us, length us, event | category | flops | bytes accessed | tf_op | source)
XLA Modules:
  0.0 609.4 jit_solution(10289231182906690298)
XLA Ops:
  7.2 4.4 collective-permute-start.2
  11.6 4.6 collective-permute-start.6
  16.2 8.1 %all-to-all-start = ((bf16[1,8,2,32,256]{4,3,2,0,1:T(8,128)(2,1)}), bf16[1,8,2,32,256]{4,3,2,0,1:T(8,128)(2,1)S(1)}, u32[]{:S(2)}, u32[]{:S(2)}) async-start(bf16[1,8,2,32,256]{4,3,2,0,1:T(8,128)(2,1)} %bitcast.2020), calls=%async_computation | async-start | bytes 524288 | tf_op jit(solution)/shard_map/all_to_all | solution.py:140
  24.3 3.4 collective-permute-start.3
  31.4 3.2 collective-permute-start.4
  35.9 3.1 collective-permute-start.7
  41.8 27.8 %all_gather.3 = bf16[8,3,32,32]{3,2,0,1:T(8,128)(2,1)S(1)} all-gather(bf16[1,3,32,32]{3,2,0,1:T(8,128)(2,1)} %bitcast.2021), channel_id=1, replica_groups=mesh['segment'=8,'gy'=64] {'segment'}, dimensions={0}, use_global_device_ids=true | all-gather | bytes 55296 | tf_op jit(solution)/shard_map/all_gather | solution.py:142
  71.6 4.2 collective-permute-done.8
  78.9 3.5 collective-permute-done.1
  87.1 3.5 collective-permute-start.9
  96.4 3.5 collective-permute-start.12
  102.9 3.8 collective-permute-done.11
  108.6 3.2 collective-permute-start.13
  113.3 5.0 collective-permute-done.14
  120.4 5.6 collective-permute-start.16
  128.6 4.4 collective-permute-done.15
  134.9 3.2 collective-permute-start.17
  144.0 3.9 collective-permute-start.20
  150.5 3.2 collective-permute-done.19
  155.5 3.0 collective-permute-start.21
  164.6 3.1 collective-permute-start.24
  175.4 3.0 collective-permute-start.25
  184.5 3.1 collective-permute-start.28
  195.3 3.0 collective-permute-start.29
  204.5 3.1 collective-permute-start.32
  215.3 3.0 collective-permute-start.33
  219.8 3.8 collective-permute-done.34
  225.6 3.1 collective-permute-start.36
  241.0 3.6 collective-permute-done.38
  246.7 3.1 collective-permute-start.40
  268.4 84.7 %all-reduce.20.cloned.1.call-done = f32[8,12288]{1,0:T(8,128)} async-done(((f32[8,12288]{1,0:T(8,128)}), f32[8,12288]{1,0:T(8,128)}) %all-reduce.20.cloned.1.call-update) | async-done | bytes 393232
  354.8 246.2 %psum.7 = f32[1,12288]{1,0:T(1,128)S(1)} all-reduce(f32[1,12288]{1,0:T(1,128)S(1)} %constant_dynamic-slice_fusion), channel_id=1, replica_groups=mesh['segment'=8,'gy'=64] {'gy'}, use_global_device_ids=true, to_apply=%region_2.3 | all-reduce | flops 12288 | bytes 98304 | tf_op jit(solution)/shard_map/psum | solution.py:170
  (367 shorter events, 126.7 us)
Async XLA Ops:
  7.2 17.2 %collective-permute-start.2 = (bf16[1,3,3,32,32]{4,3,0,2,1:T(8,128)(2,1)}, bf16[1,3,3,32,32]{4,3,0,2,1:T(8,128)(2,1)S(1)}, u32[]{:S(2)}, u32[]{:S(2)}) collective-permute-start(bf16[1,3,3,32,32]{4,3,0,2,1:T(8,128)(2,1)} %bitcast.2018), channel_id=1, source_target_pairs={{0,64},{64,128},{128,192},{192,256},{256,320},{320,384},{384,448},... | collective-permute-start | bytes 55304 | tf_op jit(solution)/shard_map/ppermute | solution.py:16
  11.6 24.3 %collective-permute-start.6 = (bf16[1,3,3,32,32]{4,3,0,2,1:T(8,128)(2,1)}, bf16[1,3,3,32,32]{4,3,0,2,1:T(8,128)(2,1)S(1)}, u32[]{:S(2)}, u32[]{:S(2)}) collective-permute-start(bf16[1,3,3,32,32]{4,3,0,2,1:T(8,128)(2,1)} %bitcast.2019), channel_id=1, source_target_pairs={{0,448},{64,0},{128,64},{192,128},{256,192},{320,256},{384,320},{4... | collective-permute-start | bytes 55304 | tf_op jit(solution)/shard_map/ppermute | solution.py:18
  16.2 59.9 %all-to-all-start = ((bf16[1,8,2,32,256]{4,3,2,0,1:T(8,128)(2,1)}), bf16[1,8,2,32,256]{4,3,2,0,1:T(8,128)(2,1)S(1)}, u32[]{:S(2)}, u32[]{:S(2)}) async-start(bf16[1,8,2,32,256]{4,3,2,0,1:T(8,128)(2,1)} %bitcast.2020), calls=%async_computation | async-start | bytes 524288 | tf_op jit(solution)/shard_map/all_to_all | solution.py:140
  24.3 328.8 %all-reduce.20.cloned.1.call-start = ((), (), s32[]{:S(2)}) async-start(), calls=%async_computation.1 | async-start | bytes 786432
  24.3 7.1 %collective-permute-start.3 = (bf16[1,3,3,32,32]{4,3,0,2,1:T(8,128)(2,1)S(1)}, bf16[1,3,3,32,32]{4,3,0,2,1:T(8,128)(2,1)S(1)}, u32[]{:S(2)}, u32[]{:S(2)}) collective-permute-start(bf16[1,3,3,32,32]{4,3,0,2,1:T(8,128)(2,1)S(1)} %collective-permute-done.2), channel_id=1, source_target_pairs={{0,64},{64,128},{128,192},{192,256},{256,320},{320,384},{384,448},... | collective-permute-start | bytes 55304 | tf_op jit(solution)/shard_map/ppermute | solution.py:16
  31.4 7.6 %collective-permute-start.4 = (bf16[1,3,3,32,32]{4,3,0,2,1:T(8,128)(2,1)S(1)}, bf16[1,3,3,32,32]{4,3,0,2,1:T(8,128)(2,1)S(1)}, u32[]{:S(2)}, u32[]{:S(2)}) collective-permute-start(bf16[1,3,3,32,32]{4,3,0,2,1:T(8,128)(2,1)S(1)} %collective-permute-done.3), channel_id=1, source_target_pairs={{0,64},{64,128},{128,192},{192,256},{256,320},{320,384},{384,448},... | collective-permute-start | bytes 55304 | tf_op jit(solution)/shard_map/ppermute | solution.py:16
  35.9 33.6 %collective-permute-start.7 = (bf16[1,3,3,32,32]{4,3,0,2,1:T(8,128)(2,1)S(1)}, bf16[1,3,3,32,32]{4,3,0,2,1:T(8,128)(2,1)S(1)}, u32[]{:S(2)}, u32[]{:S(2)}) collective-permute-start(bf16[1,3,3,32,32]{4,3,0,2,1:T(8,128)(2,1)S(1)} %collective-permute-done.6), channel_id=1, source_target_pairs={{0,448},{64,0},{128,64},{192,128},{256,192},{320,256},{384,320},{4... | collective-permute-start | bytes 55304 | tf_op jit(solution)/shard_map/ppermute | solution.py:18
  39.1 32.4 %collective-permute-start.5 = (bf16[1,3,3,32,32]{4,3,0,2,1:T(8,128)(2,1)S(1)}, bf16[1,3,3,32,32]{4,3,0,2,1:T(8,128)(2,1)S(1)}, u32[]{:S(2)}, u32[]{:S(2)}) collective-permute-start(bf16[1,3,3,32,32]{4,3,0,2,1:T(8,128)(2,1)S(1)} %collective-permute-done.4), channel_id=1, source_target_pairs={{0,64},{64,128},{128,192},{192,256},{256,320},{320,384},{384,448},... | collective-permute-start | bytes 55304 | tf_op jit(solution)/shard_map/ppermute | solution.py:16
  69.6 6.2 %collective-permute-start.8 = (bf16[1,3,3,32,32]{4,3,0,2,1:T(8,128)(2,1)S(1)}, bf16[1,3,3,32,32]{4,3,0,2,1:T(8,128)(2,1)S(1)}, u32[]{:S(2)}, u32[]{:S(2)}) collective-permute-start(bf16[1,3,3,32,32]{4,3,0,2,1:T(8,128)(2,1)S(1)} %collective-permute-done.7), channel_id=1, source_target_pairs={{0,448},{64,0},{128,64},{192,128},{256,192},{320,256},{384,320},{4... | collective-permute-start | bytes 55304 | tf_op jit(solution)/shard_map/ppermute | solution.py:18
  84.7 8.4 %collective-permute-start.10 = (bf16[8,1,2,32,256]{4,3,2,0,1:T(8,128)(2,1)S(1)}, bf16[8,1,2,32,256]{4,3,2,0,1:T(8,128)(2,1)S(1)}, u32[]{:S(2)}, u32[]{:S(2)}) collective-permute-start(bf16[8,1,2,32,256]{4,3,2,0,1:T(8,128)(2,1)S(1)} %bitcast.2001), channel_id=1, source_target_pairs={{64,0},{128,64},{192,128},{256,192},{320,256},{384,320},{448,384},... | collective-permute-start | bytes 786440 | tf_op jit(solution)/shard_map/ppermute | solution.py:31
  87.1 8.7 %collective-permute-start.9 = (bf16[8,1,2,32,256]{4,3,2,0,1:T(8,128)(2,1)S(1)}, bf16[8,1,2,32,256]{4,3,2,0,1:T(8,128)(2,1)S(1)}, u32[]{:S(2)}, u32[]{:S(2)}) collective-permute-start(bf16[8,1,2,32,256]{4,3,2,0,1:T(8,128)(2,1)S(1)} %bitcast.2002), channel_id=1, source_target_pairs={{0,64},{64,128},{128,192},{192,256},{256,320},{320,384},{384,448},... | collective-permute-start | bytes 786440 | tf_op jit(solution)/shard_map/ppermute | solution.py:28
  96.4 6.3 %collective-permute-start.12 = (bf16[1,2,32,256]{3,2,1,0:T(8,128)(2,1)S(1)}, bf16[1,2,32,256]{3,2,1,0:T(8,128)(2,1)S(1)}, u32[]{:S(2)}, u32[]{:S(2)}) collective-permute-start(bf16[1,2,32,256]{3,2,1,0:T(8,128)(2,1)S(1)} %fusion.97), channel_id=1, source_target_pairs={{0,64},{64,128},{128,192},{192,256},{256,320},{320,384},{384,448},... | collective-permute-start | bytes 98312 | tf_op jit(solution)/shard_map/ppermute | solution.py:28
  99.9 6.8 %collective-permute-start.11 = (bf16[1,2,32,256]{3,2,1,0:T(8,128)(2,1)S(1)}, bf16[1,2,32,256]{3,2,1,0:T(8,128)(2,1)S(1)}, u32[]{:S(2)}, u32[]{:S(2)}) collective-permute-start(bf16[1,2,32,256]{3,2,1,0:T(8,128)(2,1)S(1)} %fusion.97), channel_id=1, source_target_pairs={{64,0},{128,64},{192,128},{256,192},{320,256},{384,320},{448,384},... | collective-permute-start | bytes 98312 | tf_op jit(solution)/shard_map/ppermute | solution.py:31
  111.8 6.5 %collective-permute-start.14 = (bf16[1,1,32,256]{3,2,1,0:T(8,128)(2,1)S(1)}, bf16[1,1,32,256]{3,2,1,0:T(8,128)(2,1)S(1)}, u32[]{:S(2)}, u32[]{:S(2)}) collective-permute-start(bf16[1,1,32,256]{3,2,1,0:T(8,128)(2,1)S(1)} %get-tuple-element.36), channel_id=1, source_target_pairs={{1,0},{2,1},{3,2},{4,3},{5,4},{6,5},{7,6},{8,7},{9,8},{10,9},{11,1... | collective-permute-start | bytes 49160 | tf_op jit(solution)/shard_map/ppermute | solution.py:31
  120.4 8.0 %collective-permute-start.16 = (bf16[1,2,32,256]{3,2,1,0:T(8,128)(2,1)S(1)}, bf16[1,2,32,256]{3,2,1,0:T(8,128)(2,1)S(1)}, u32[]{:S(2)}, u32[]{:S(2)}) collective-permute-start(bf16[1,2,32,256]{3,2,1,0:T(8,128)(2,1)S(1)} %get-tuple-element.37), channel_id=1, source_target_pairs={{0,64},{64,128},{128,192},{192,256},{256,320},{320,384},{384,448},... | collective-permute-start | bytes 98312 | tf_op jit(solution)/shard_map/ppermute | solution.py:28
  126.0 7.0 %collective-permute-start.15 = (bf16[1,2,32,256]{3,2,1,0:T(8,128)(2,1)S(1)}, bf16[1,2,32,256]{3,2,1,0:T(8,128)(2,1)S(1)}, u32[]{:S(2)}, u32[]{:S(2)}) collective-permute-start(bf16[1,2,32,256]{3,2,1,0:T(8,128)(2,1)S(1)} %get-tuple-element.37), channel_id=1, source_target_pairs={{64,0},{128,64},{192,128},{256,192},{320,256},{384,320},{448,384},... | collective-permute-start | bytes 98312 | tf_op jit(solution)/shard_map/ppermute | solution.py:31
  144.0 6.3 %collective-permute-start.20 = (bf16[1,2,32,256]{3,2,1,0:T(8,128)(2,1)S(1)}, bf16[1,2,32,256]{3,2,1,0:T(8,128)(2,1)S(1)}, u32[]{:S(2)}, u32[]{:S(2)}) collective-permute-start(bf16[1,2,32,256]{3,2,1,0:T(8,128)(2,1)S(1)} %get-tuple-element.39), channel_id=1, source_target_pairs={{0,64},{64,128},{128,192},{192,256},{256,320},{320,384},{384,448},... | collective-permute-start | bytes 98312 | tf_op jit(solution)/shard_map/ppermute | solution.py:28
  147.9 5.8 collective-permute-start.19
  164.6 6.3 %collective-permute-start.24 = (bf16[1,2,32,256]{3,2,1,0:T(8,128)(2,1)S(1)}, bf16[1,2,32,256]{3,2,1,0:T(8,128)(2,1)S(1)}, u32[]{:S(2)}, u32[]{:S(2)}) collective-permute-start(bf16[1,2,32,256]{3,2,1,0:T(8,128)(2,1)S(1)} %get-tuple-element.41), channel_id=1, source_target_pairs={{0,64},{64,128},{128,192},{192,256},{256,320},{320,384},{384,448},... | collective-permute-start | bytes 98312 | tf_op jit(solution)/shard_map/ppermute | solution.py:28
  167.8 5.8 collective-permute-start.23
  184.5 6.3 %collective-permute-start.28 = (bf16[1,2,32,256]{3,2,1,0:T(8,128)(2,1)S(1)}, bf16[1,2,32,256]{3,2,1,0:T(8,128)(2,1)S(1)}, u32[]{:S(2)}, u32[]{:S(2)}) collective-permute-start(bf16[1,2,32,256]{3,2,1,0:T(8,128)(2,1)S(1)} %get-tuple-element.43), channel_id=1, source_target_pairs={{0,64},{64,128},{128,192},{192,256},{256,320},{320,384},{384,448},... | collective-permute-start | bytes 98312 | tf_op jit(solution)/shard_map/ppermute | solution.py:28
  187.6 5.8 collective-permute-start.27
  204.5 6.3 %collective-permute-start.32 = (bf16[1,2,32,256]{3,2,1,0:T(8,128)(2,1)S(1)}, bf16[1,2,32,256]{3,2,1,0:T(8,128)(2,1)S(1)}, u32[]{:S(2)}, u32[]{:S(2)}) collective-permute-start(bf16[1,2,32,256]{3,2,1,0:T(8,128)(2,1)S(1)} %get-tuple-element.45), channel_id=1, source_target_pairs={{0,64},{64,128},{128,192},{192,256},{256,320},{320,384},{384,448},... | collective-permute-start | bytes 98312 | tf_op jit(solution)/shard_map/ppermute | solution.py:28
  207.7 5.8 collective-permute-start.31
  218.3 5.2 collective-permute-start.34
  225.6 6.3 %collective-permute-start.36 = (bf16[1,2,32,256]{3,2,1,0:T(8,128)(2,1)S(1)}, bf16[1,2,32,256]{3,2,1,0:T(8,128)(2,1)S(1)}, u32[]{:S(2)}, u32[]{:S(2)}) collective-permute-start(bf16[1,2,32,256]{3,2,1,0:T(8,128)(2,1)S(1)} %get-tuple-element.47), channel_id=1, source_target_pairs={{0,64},{64,128},{128,192},{192,256},{256,320},{320,384},{384,448},... | collective-permute-start | bytes 98312 | tf_op jit(solution)/shard_map/ppermute | solution.py:28
  228.7 5.8 collective-permute-start.35
  239.3 5.2 collective-permute-start.38
  246.7 6.5 %collective-permute-start.40 = (bf16[1,2,32,256]{3,2,1,0:T(8,128)(2,1)S(1)}, bf16[1,2,32,256]{3,2,1,0:T(8,128)(2,1)S(1)}, u32[]{:S(2)}, u32[]{:S(2)}) collective-permute-start(bf16[1,2,32,256]{3,2,1,0:T(8,128)(2,1)S(1)} %get-tuple-element.49), channel_id=1, source_target_pairs={{0,64},{64,128},{128,192},{192,256},{256,320},{320,384},{384,448},... | collective-permute-start | bytes 98312 | tf_op jit(solution)/shard_map/ppermute | solution.py:28
  249.8 5.8 collective-permute-start.39
  257.6 5.6 collective-permute-start.41
  260.6 5.2 collective-permute-start.42
  (15 other events, 122.9 us)
Sparse Core Ops, SparseCore 0:
  263.4 89.7 all-reduce.19
